TPU v7x, 32 devices: a whole 2x2x4 slice. The times are simulated.
32 devices in a mesh: dp: 4 (over y, x), expert: 8 (over z, core).
Axes of the slice: x: 2, y: 2, z: 4, core: 2. Of those that a mesh axis runs over, the one named last changes fastest.
Arguments:
- context: bfloat16 [8, 4, 128, 1536], P('expert', None, None, 'dp'), may hold values from -0.29882812 to 0.29882812
- w_proj: bfloat16 [1536, 1536], P('dp'), may hold values from -0.15625 to 0.15625
- residual: bfloat16 [4096, 1536], P(('dp', 'expert')), may hold values from -0.29882812 to 0.29882812
- gain_first: float32 [1536], replicated, may hold values from 0.25 to 1.75
- gain_next: float32 [1536], replicated, may hold values from 0.25 to 1.75
- w_router: bfloat16 [1536, 40], replicated, may hold values from -0.15625 to 0.15625
- expert_ids: int32 [4096, 8], P(('dp', 'expert')), may hold values from 0 to 39, all different within a row
- replica_pick: int32 [4096, 8], P(('dp', 'expert')), may hold values from 0 to 5039
- slot_expert: int32 [48], replicated, may hold values from 0 to 39, as said below
- cap_blocks: int32 [48], replicated, may hold values from 1 to 4
- w_in: bfloat16 [48, 1536, 1024], P('expert', 'dp'), as said below
- w_out: bfloat16 [48, 512, 1536], P('expert', 'dp'), as said below
Outputs:
- residual_out: bfloat16 [4096, 1536], P(('dp', 'expert'))
- next_normed: bfloat16 [4096, 1536], P(('dp', 'expert'))
Inputs may be any that keep to these rules, and one draw needn't show every extreme that they name: `slot_expert`: every expert is held by at least one slot; slot s lies on index s // 6 of the expert axis. `w_in`: two slots that hold the same expert have equal weights. `w_out`: two slots that hold the same expert have equal weights.
All inputs are finite; a program needn't handle non-finite values.
Results may differ from a plain program's by a relative error of at most 0.01.
Values may be sent and summed in bfloat16 or wider, within the bound.
No kernel may reach another device: no remote copies, remote signals or barrier semaphores. Data moves between devices by JAX's collectives and lax.ppermute only.
A program may use at most 128 MiB of HBM per device.

v0:
```python
import jax
import jax.numpy as jnp
from jax import lax
from jax.sharding import PartitionSpec as P

CAP_UNIT = 8
CAP_MOST = 32


def rms_scale(values, gain):
    widened = values.astype(jnp.float32)
    return widened * lax.rsqrt(jnp.mean(widened * widened, axis=-1, keepdims=True) + 1e-06) * gain


def route_rows(
    normed, w_router, expert_ids, replica_pick, slot_expert, cap_blocks, groups, cap_unit
):
    row_count = normed.shape[0]
    experts_all = w_router.shape[1]
    slots_all = slot_expert.shape[0]
    topk_all = expert_ids.shape[1]
    logits = jnp.dot(normed, w_router, preferred_element_type=jnp.float32)
    expert_axis = jnp.arange(experts_all)
    one_hot = expert_ids[:, :, None] == expert_axis
    chosen = jnp.sum(jnp.where(one_hot, logits[:, None, :], jnp.float32(0.0)), axis=-1)
    raised = jnp.exp(chosen)
    gates = raised / jnp.sum(raised, axis=-1, keepdims=True)
    holder = (slot_expert[None, :] == expert_axis[:, None]).astype(jnp.int32)
    rep_count = jnp.sum(holder, axis=1)
    earlier = jnp.cumsum(holder, axis=1) - holder
    slot_rank = jnp.sum(earlier * holder, axis=0)
    count_of = jnp.sum(jnp.where(one_hot, rep_count, 0), axis=-1)
    replica = replica_pick % count_of
    slot_axis = jnp.arange(slots_all)
    matched = (slot_expert == expert_ids[:, :, None]) & (slot_rank == replica[:, :, None])
    target_slot = jnp.sum(jnp.where(matched, slot_axis, 0), axis=-1)
    selected = matched.astype(jnp.int32).reshape(groups, -1, slots_all)
    before = jnp.cumsum(selected, axis=1) - selected
    position = jnp.sum(before * selected, axis=-1).reshape(row_count, topk_all)
    capacity = (
        jnp.sum(jnp.where(target_slot[:, :, None] == slot_axis, cap_blocks, 0), axis=-1) * cap_unit
    )
    retained = position < capacity
    return (gates, target_slot, position, retained)


def on_device(
    context,
    w_proj,
    residual,
    gain_first,
    gain_next,
    w_router,
    expert_ids,
    replica_pick,
    slot_expert,
    cap_blocks,
    w_in,
    w_out,
):
    tok_rows = residual.shape[0]
    model_width = residual.shape[1]
    topk_all = expert_ids.shape[1]
    slots_all = slot_expert.shape[0]
    slot_local = w_in.shape[0]
    expert_count = lax.axis_size("expert")
    full_in, full_out = (
        lax.all_gather(w_in, "dp", axis=1, tiled=True),
        lax.all_gather(w_out, "dp", axis=1, tiled=True),
    )
    hidden_units = full_in.shape[2] // 2
    flat_context = context.reshape(-1, context.shape[3])
    attended = lax.psum_scatter(
        jnp.dot(flat_context, w_proj, preferred_element_type=jnp.float32),
        "dp",
        scatter_dimension=0,
        tiled=True,
    )
    hidden_state = (residual.astype(jnp.float32) + attended).astype(jnp.bfloat16)
    normed = rms_scale(hidden_state, gain_first).astype(jnp.bfloat16)
    gates, target_slot, position, retained = route_rows(
        normed, w_router, expert_ids, replica_pick, slot_expert, cap_blocks, 1, CAP_UNIT
    )
    target = jnp.where(retained, position, CAP_MOST)
    spread_rows = jnp.broadcast_to(normed[:, None, :], (tok_rows, topk_all, model_width))
    outgoing = (
        jnp.zeros((slots_all, CAP_MOST, model_width), jnp.bfloat16)
        .at[target_slot, target]
        .set(spread_rows, mode="drop")
    )
    received = lax.all_to_all(outgoing, "expert", split_axis=0, concat_axis=0, tiled=True)
    received = received.reshape(expert_count, slot_local, CAP_MOST, model_width)
    gate_up = jnp.einsum("jsrd,sdf->jsrf", received, full_in, preferred_element_type=jnp.float32)
    activated = (jax.nn.silu(gate_up[..., :hidden_units]) * gate_up[..., hidden_units:]).astype(
        jnp.bfloat16
    )
    expert_out = jnp.einsum(
        "jsrf,sfd->jsrd", activated, full_out, preferred_element_type=jnp.float32
    ).astype(jnp.bfloat16)
    expert_out = expert_out.reshape(slots_all, CAP_MOST, model_width)
    returned = lax.all_to_all(expert_out, "expert", split_axis=0, concat_axis=0, tiled=True)
    clipped = jnp.minimum(position, CAP_MOST - 1)
    picked = returned[target_slot, clipped]
    weighting = jnp.where(retained, gates, jnp.float32(0.0))
    combined = jnp.sum(weighting[:, :, None] * picked.astype(jnp.float32), axis=1)
    residual_out = (hidden_state.astype(jnp.float32) + combined).astype(jnp.bfloat16)
    next_normed = rms_scale(residual_out, gain_next).astype(jnp.bfloat16)
    return (residual_out, next_normed)


def solution(mesh):
    placed = (
        P("expert", None, None, "dp"),
        P("dp", None),
        P(("dp", "expert"), None),
        P(),
        P(),
        P(),
        P(("dp", "expert"), None),
        P(("dp", "expert"), None),
        P(),
        P(),
        P("expert", "dp", None),
        P("expert", "dp", None),
    )
    return jax.shard_map(
        on_device,
        mesh=mesh,
        in_specs=placed,
        out_specs=(P(("dp", "expert"), None), P(("dp", "expert"), None)),
        check_vma=False,
    )
```

profile of v0, /device:TPU:0, one launch (start us, length us, event | category | flops | bytes accessed | tf_op | source)
XLA Modules:
  0.0 491.6 jit_solution(5937265904727964733)
XLA Ops:
  7.2 0.0 copy-start
  7.2 0.0 reduce-scatter.2.cloned.1.call-start
  7.2 1.2 copy-done
  8.4 3.7 fusion.36
  12.2 0.0 reduce-scatter.2.cloned.1.call-update
  12.2 0.0 copy-start.10
  12.2 0.0 copy-start.12
  12.2 0.0 copy-start.11
  12.2 0.0 copy-start.3
  12.2 0.0 all-gather.3.cloned.1.call-start
  12.3 0.7 all-gather.3.cloned.1.call-update
  13.0 0.0 copy-start.7
  13.0 0.0 all-gather.5.cloned.1.call-start
  13.1 0.7 all-gather.5.cloned.1.call-update
  13.7 0.0 copy-done.5
  13.8 0.1 copy.53
  13.9 0.0 copy-done.6
  13.9 0.2 reduce_window_sum.31
  14.1 0.1 select_reduce_fusion.4
  14.2 0.1 select_reduce_fusion.3
  14.3 0.0 copy-done.9
  14.3 0.1 add_select_fusion
  14.4 0.1 copy.54
  14.5 0.1 eq.117
  14.6 0.1 eq.106
  14.7 0.1 convert_bitcast_fusion.1
  14.9 13.5 %reduce-window.6 = s32[1,48,8,128]{3,2,1,0:T(8,128)S(1)} reduce-window(s32[1,48,8,128]{3,2,1,0:T(8,128)S(1)} %bitcast.57, s32[]{:T(128)} %constant.11.clone.1), window={size=1x1x1x128 pad=0_0x0_0x0_0x127_0}, to_apply=%region_5.6 | reduce-window | flops 6242304 | bytes 393220 | tf_op jit(solution)/shard_map/reduce-window
  28.4 0.1 slice.18
  28.6 0.1 copy.55
  28.7 0.1 copy.56
  28.8 0.1 broadcast.256
  29.0 0.1 fusion.28
  29.1 0.1 reshape.345
  29.2 0.1 select_reduce_fusion.1
  29.4 0.0 copy-done.10
  29.4 0.1 select_reduce_fusion
  29.5 0.1 multiply_reduce_fusion
  29.6 0.1 and_reduce_fusion
  29.7 0.1 copy.61
  29.8 0.1 reshape.358
  29.9 29.2 %reduce-scatter.2.cloned.1.call-done = f32[128,1536]{1,0:T(8,128)} async-done(((f32[512,1536]{1,0:T(8,128)}), f32[128,1536]{1,0:T(8,128)}) %reduce-scatter.2.cloned.1.call-update) | async-done | bytes 786448 | tf_op jit(solution)/shard_map/reduce_scatter | solution.py:73
  59.1 0.0 copy-done.3
  59.1 1.3 fusion.23
  60.4 0.2 fusion.25
  60.6 9.2 %scatter_custom_fusion = bf16[1536,1536]{1,0:T(8,128)(2,1)} fusion(s32[1024]{0:T(1024)S(1)} %reshape.358, bf16[]{:T(256)} %constant.33.clone.1, bf16[128,1536]{1,0:T(8,128)(2,1)S(1)} %fusion.25), kind=kCustom, calls=%fused_computation.12 | custom fusion | bytes 5111810
  69.8 109.9 %all_to_all.10 = bf16[48,32,1536]{2,1,0:T(8,128)(2,1)} all-to-all(bf16[48,32,1536]{2,1,0:T(8,128)(2,1)} %bitcast.54), channel_id=1, replica_groups=mesh['dp'=4,'expert'=8] {'expert'}, dimensions={0} | all-to-all | bytes 9437184 | tf_op jit(solution)/shard_map/all_to_all | solution.py:91
  179.7 56.9 %all-gather.3.cloned.1.call-done = bf16[6,1536,1024]{2,1,0:T(8,128)(2,1)} async-done(((bf16[6,384,1024]{2,1,0:T(8,128)(2,1)}), bf16[6,1536,1024]{2,1,0:T(8,128)(2,1)}) %all-gather.3.cloned.1.call-update) | async-done | bytes 18874384 | tf_op jit(solution)/shard_map/all_gather | solution.py:68
  236.6 12.1 %fusion.11 = f32[8,6,32,1024]{3,2,0,1:T(8,128)} fusion(bf16[6,1536,1024]{2,1,0:T(8,128)(2,1)} %all-gather.3.cloned.1.call-done, bf16[8,6,32,1536]{3,2,1,0:T(8,128)(2,1)} %bitcast.55), kind=kOutput, calls=%fused_computation.14 | convolution fusion | flops 4831838208 | bytes 29884416 | tf_op jit(solution)/shard_map/jsrd,sdf->jsrf/dot_general | solution.py:93
  248.7 86.0 %all-gather.5.cloned.1.call-done = bf16[6,512,1536]{2,1,0:T(8,128)(2,1)} async-done(((bf16[6,128,1536]{2,1,0:T(8,128)(2,1)}), bf16[6,512,1536]{2,1,0:T(8,128)(2,1)}) %all-gather.5.cloned.1.call-update) | async-done | bytes 9437200 | tf_op jit(solution)/shard_map/all_gather | solution.py:69
  334.7 8.2 %convert_bitcast_fusion = bf16[8,6,32,1536]{3,2,0,1:T(8,128)(2,1)S(1)} fusion(bf16[6,512,1536]{2,1,0:T(8,128)(2,1)} %all-gather.5.cloned.1.call-done, f32[8,6,32,1024]{3,2,0,1:T(8,128)} %fusion.11), kind=kOutput, calls=%fused_computation.9 | convolution fusion | flops 2422996992 | bytes 20447232 | tf_op jit(solution)/shard_map/jsrf,sfd->jsrd/dot_general | solution.py:97
  342.9 2.5 copy.63
  345.4 4.9 all-to-all-start.1
  350.3 0.1 reshape.344
  350.4 0.1 copy.65
  350.5 0.1 reshape.352
  350.6 0.2 fusion.37
  350.9 0.1 select_reduce_fusion.2
  351.0 0.1 copy.58
  351.1 104.5 %all-to-all-done.1 = bf16[48,32,1536]{2,1,0:T(8,128)(2,1)} async-done(((bf16[48,32,1536]{2,1,0:T(8,128)(2,1)}), bf16[48,32,1536]{2,1,0:T(8,128)(2,1)}, u32[]{:S(2)}, u32[]{:S(2)}) %all-to-all-start.1) | async-done | bytes 4718624 | tf_op jit(solution)/shard_map/all_to_all | solution.py:101
  455.5 23.6 %gather_fusion = bf16[1024,1536]{1,0:T(8,128)(2,1)} fusion(bf16[48,32,1536]{2,1,0:T(8,128)(2,1)} %all-to-all-done.1, s32[1024]{0:T(1024)S(1)} %reshape.352), kind=kCustom, calls=%fused_computation | custom fusion | bytes 6299648 | tf_op jit(solution)/shard_map/gather | solution.py:103
  479.1 4.7 fusion.4
  483.9 0.2 fusion.20
  484.1 0.9 fusion.22
  485.0 0.0 copy-done.1
  (27 shorter events, 0.3 us)
Async XLA Ops:
  7.2 1.3 copy-start
  7.2 51.9 %reduce-scatter.2.cloned.1.call-start = ((), (), s32[]{:S(2)}) async-start(), calls=%async_computation.3 | async-start | bytes 3932160 | tf_op jit(solution)/shard_map/reduce_scatter | solution.py:73
  12.2 1.6 copy-start.5
  12.2 1.7 copy-start.6
  12.2 2.1 copy-start.9
  12.2 17.2 %copy-start.10 = (s32[48]{0:T(128)S(1)}, s32[48]{0:T(128)}, u32[]{:S(2)}) copy-start(s32[48]{0:T(128)} %param.21) | copy-start | bytes 580
  12.2 17.3 %copy-start.12 = (s32[2]{0:T(128)S(1)}, s32[2]{0:T(128)}, u32[]{:S(2)}) copy-start(s32[2]{0:T(128)} %constant.41) | copy-start | bytes 28
  12.2 17.4 %copy-start.11 = (s32[2]{0:T(128)S(1)}, s32[2]{0:T(128)}, u32[]{:S(2)}) copy-start(s32[2]{0:T(128)} %constant.44) | copy-start | bytes 28
  12.2 46.9 %copy-start.3 = (bf16[128,1536]{1,0:T(8,128)(2,1)S(1)}, bf16[128,1536]{1,0:T(8,128)(2,1)}, u32[]{:S(2)}) copy-start(bf16[128,1536]{1,0:T(8,128)(2,1)} %param.14) | copy-start | bytes 1179652
  12.2 224.4 %all-gather.3.cloned.1.call-start = ((), (), s32[]{:S(2)}) async-start(), calls=%async_computation.4 | async-start | bytes 23592960 | tf_op jit(solution)/shard_map/all_gather | solution.py:68
  13.0 47.4 %copy-start.7 = (f32[1536]{0:T(1024)S(1)}, f32[1536]{0:T(1024)}, u32[]{:S(2)}) copy-start(f32[1536]{0:T(1024)} %param.15) | copy-start | bytes 18436
  13.0 321.7 %all-gather.5.cloned.1.call-start = ((), (), s32[]{:S(2)}) async-start(), calls=%async_computation.5 | async-start | bytes 11796480 | tf_op jit(solution)/shard_map/all_gather | solution.py:69
  345.4 5.2 %copy-start.4 = (bf16[1536,40]{0,1:T(8,128)(2,1)S(1)}, bf16[1536,40]{0,1:T(8,128)(2,1)}, u32[]{:S(2)}) copy-start(bf16[1536,40]{0,1:T(8,128)(2,1)} %param.17) | copy-start | bytes 368644
  345.4 110.1 %all-to-all-start.1 = ((bf16[48,32,1536]{2,1,0:T(8,128)(2,1)}), bf16[48,32,1536]{2,1,0:T(8,128)(2,1)}, u32[]{:S(2)}, u32[]{:S(2)}) async-start(bf16[48,32,1536]{2,1,0:T(8,128)(2,1)} %bitcast.53), calls=%async_computation.2 | async-start | bytes 9437184 | tf_op jit(solution)/shard_map/all_to_all | solution.py:101
  455.5 29.5 %copy-start.1 = (bf16[384,1536]{1,0:T(8,128)(2,1)S(1)}, bf16[384,1536]{1,0:T(8,128)(2,1)}, u32[]{:S(2)}) copy-start(bf16[384,1536]{1,0:T(8,128)(2,1)} %param.13) | copy-start | bytes 3538948
  479.1 5.0 %copy-start.8 = (f32[1536]{0:T(1024)S(1)}, f32[1536]{0:T(1024)}, u32[]{:S(2)}) copy-start(f32[1536]{0:T(1024)} %param.16) | copy-start | bytes 18436
  484.1 0.9 copy-start.2
Sparse Core Ops, SparseCore 0:
  12.3 46.7 reduce-scatter.1
  60.9 175.6 all-gather.2
  238.5 96.1 all-gather.4
where the time goes:
time: 492 us
  waiting for transfers between devices  278 us (57%)
  blocking collectives  110 us (22%)
  local copies, waits for them, and re-layouts  38.3 us (8%)
  matrix products  24.3 us (5%)
  other arithmetic  22.1 us (4%)
  between operations  14 us (3%)
  starting transfers between devices  5.02 us (1%)
    all_to_all x1, blocking collectives, on_device(): lax.all_to_all(outgoing, 'expert', split_axis=0, concat_axis=0, tiled=True)  110 us
    all_to_all x1, waiting for transfers between devices, on_device(): lax.all_to_all(expert_out, 'expert', split_axis=0, concat_axis=0, tiled=T...  104 us
    all_gather x1, waiting for transfers between devices, on_device(): lax.all_gather(w_out, 'dp', axis=1, tiled=True)  86 us
    all_gather x1, waiting for transfers between devices, on_device(): lax.all_gather(w_in, 'dp', axis=1, tiled=True)  56.9 us
    reduce_scatter x1, waiting for transfers between devices, on_device(): lax.psum_scatter(jnp.dot(flat_context, w_proj, preferred_element_type=jnp...  29.2 us
    gather x1, local copies, waits for them, and re-layouts, on_device(): picked = returned[target_slot, clipped]  23.6 us
    another operation x2, other arithmetic  13.5 us
    dot_general x1, matrix products, on_device(): jnp.einsum('jsrd,sdf->jsrf', received, full_in, preferred_element_type=jn...  12.1 us
  transfers between devices with their start and end apart: 4, of which 4 were waited for; matrix products, arithmetic and copies ran while one was open for 8% of the time, Pallas kernels for 0%

commit v1 on v0

--- a/solution.py
+++ b/solution.py
@@ -5,6 +5,17 @@
 
 CAP_UNIT = 8
 CAP_MOST = 32
+
+
+def ring_gather(x, axis, dim):
+    ways = lax.axis_size(axis)
+    pieces = [x]
+    for far in range(1, ways):
+        pieces.append(
+            lax.ppermute(pieces[far - 1], axis, [(d, (d - 1) % ways) for d in range(ways)])
+        )
+    line = jnp.concatenate(pieces, axis=dim)
+    return jnp.roll(line, lax.axis_index(axis) * x.shape[dim], axis=dim)
 
 
 def rms_scale(values, gain):
@@ -65,7 +76,7 @@
     slot_local = w_in.shape[0]
     expert_count = lax.axis_size("expert")
     full_in, full_out = (
-        lax.all_gather(w_in, "dp", axis=1, tiled=True),
+        ring_gather(w_in, "dp", 1),
         lax.all_gather(w_out, "dp", axis=1, tiled=True),
     )
     hidden_units = full_in.shape[2] // 2

time: 492 us -> 607 us (1.23)
  waiting for transfers between devices: 278 us -> 429 us
  blocking collectives: 110 us -> 0 us
  local copies, waits for them, and re-layouts: 38.3 us -> 79.4 us
  starting transfers between devices: 5.02 us -> 36.9 us
    ppermute x0 -> x3, waiting for transfers between devices: none -> 292 us  [ring_gather(): lax.ppermute(pieces[far - 1], axis, [(d, (d - 1) % ways) for d in range(w...]
    all_to_all x1 -> x0, blocking collectives: 110 us -> none  [on_device(): lax.all_to_all(outgoing, 'expert', split_axis=0, concat_axis=0, tiled=True)]
    all_gather x1, waiting for transfers between devices: 86 us -> 21.3 us  [on_device(): lax.all_gather(w_out, 'dp', axis=1, tiled=True)]
    all_gather x1 -> x0, waiting for transfers between devices: 56.9 us -> none  [on_device(): lax.all_gather(w_in, 'dp', axis=1, tiled=True)]
    unnamed x31 -> x42, local copies, waits for them, and re-layouts: 10.9 us -> 46.5 us
    ppermute x0 -> x3, starting transfers between devices: none -> 27.3 us  [ring_gather(): lax.ppermute(pieces[far - 1], axis, [(d, (d - 1) % ways) for d in range(w...]
    reduce_scatter x1, waiting for transfers between devices: 29.2 us -> 10.6 us  [on_device(): lax.psum_scatter(jnp.dot(flat_context, w_proj, preferred_element_type=jnp...]
  transfers between devices with their start and end apart: 4 -> 7, of which waited for: 4 -> 6; matrix products, arithmetic and copies ran while one was open for 8% -> 13% of each run, Pallas kernels for 0% -> 0%
where the time goes in v1:
time: 607 us; the launch traced here: 605 us
  waiting for transfers between devices  429 us (71%)
  local copies, waits for them, and re-layouts  79.4 us (13%)
  starting transfers between devices  36.9 us (6%)
  matrix products  24.2 us (4%)
  other arithmetic  22.1 us (4%)
  between operations  14.3 us (2%)
    ppermute x3, waiting for transfers between devices, ring_gather(): lax.ppermute(pieces[far - 1], axis, [(d, (d - 1) % ways) for d in range(w...  292 us
    all_to_all x1, waiting for transfers between devices, on_device(): lax.all_to_all(expert_out, 'expert', split_axis=0, concat_axis=0, tiled=T...  104 us
    unnamed x42, local copies, waits for them, and re-layouts  46.5 us
    ppermute x3, starting transfers between devices, ring_gather(): lax.ppermute(pieces[far - 1], axis, [(d, (d - 1) % ways) for d in range(w...  27.3 us
    gather x1, local copies, waits for them, and re-layouts, on_device(): picked = returned[target_slot, clipped]  23.6 us
    all_gather x1, waiting for transfers between devices, on_device(): lax.all_gather(w_out, 'dp', axis=1, tiled=True)  21.3 us
    another operation x2, other arithmetic  13.5 us
    dot_general x1, matrix products, on_device(): jnp.einsum('jsrd,sdf->jsrf', received, full_in, preferred_element_type=jn...  12.2 us
  transfers between devices with their start and end apart: 7, of which 6 were waited for; matrix products, arithmetic and copies ran while one was open for 13% of the time, Pallas kernels for 0%

profile of v1, /device:TPU:0, one launch (start us, length us, event | category | flops | bytes accessed | tf_op | source)
XLA Modules:
  0.0 605.5 jit_solution(9738321192811187605)
XLA Ops:
  7.2 0.0 copy-start
  7.2 0.0 reduce-scatter.2.cloned.1.call-start
  7.2 1.2 copy-done
  8.5 3.6 fusion.38
  12.1 0.0 reduce-scatter.2.cloned.1.call-update
  12.1 0.0 all-gather.2.cloned.1.call-start
  12.2 4.0 collective-permute-start
  16.2 0.0 all-gather.2.cloned.1.call-update
  16.2 0.1 copy.53
  16.3 0.2 reduce_window_sum.31
  16.5 0.1 select_reduce_fusion.4
  16.6 0.1 select_reduce_fusion.3
  16.8 0.1 add_select_fusion
  16.9 0.1 copy.54
  17.0 0.1 eq.120
  17.1 0.1 eq.109
  17.2 117.2 %collective-permute-done = bf16[6,384,1024]{2,1,0:T(8,128)(2,1)} collective-permute-done((bf16[6,384,1024]{2,1,0:T(8,128)(2,1)}, bf16[6,384,1024]{2,1,0:T(8,128)(2,1)}, u32[]{:S(2)}, u32[]{:S(2)}) %collective-permute-start) | collective-permute-done | bytes 4718624 | tf_op jit(solution)/shard_map/ppermute | solution.py:15
  134.4 3.4 collective-permute-start.1
  137.8 0.1 convert_bitcast_fusion.1
  137.9 13.5 %reduce-window.6 = s32[1,48,8,128]{3,2,1,0:T(8,128)S(1)} reduce-window(s32[1,48,8,128]{3,2,1,0:T(8,128)S(1)} %bitcast.58, s32[]{:T(128)} %constant.48.clone.1), window={size=1x1x1x128 pad=0_0x0_0x0_0x127_0}, to_apply=%region_5.6 | reduce-window | flops 6242304 | bytes 393220 | tf_op jit(solution)/shard_map/reduce-window
  151.4 0.1 slice.18
  151.6 0.1 copy.55
  151.8 0.1 copy.56
  151.8 0.1 broadcast.256
  152.0 0.1 fusion.29
  152.1 0.1 reshape.345
  152.3 0.1 select_reduce_fusion.1
  152.4 0.1 select_reduce_fusion
  152.5 0.1 multiply_reduce_fusion
  152.6 0.1 and_reduce_fusion
  152.7 0.1 copy.61
  152.8 0.1 reshape.358
  152.9 10.6 %reduce-scatter.2.cloned.1.call-done = f32[128,1536]{1,0:T(8,128)} async-done(((f32[512,1536]{1,0:T(8,128)}), f32[128,1536]{1,0:T(8,128)}) %reduce-scatter.2.cloned.1.call-update) | async-done | bytes 786448 | tf_op jit(solution)/shard_map/reduce_scatter | solution.py:84
  163.5 1.3 fusion.24
  164.9 0.2 fusion.26
  165.0 8.3 %scatter_custom_fusion = bf16[1536,1536]{1,0:T(8,128)(2,1)} fusion(s32[1024]{0:T(1024)S(1)} %reshape.358, bf16[]{:T(256)} %constant.58.clone.1, bf16[128,1536]{1,0:T(8,128)(2,1)S(1)} %fusion.26), kind=kCustom, calls=%fused_computation.13 | custom fusion | bytes 5111810
  173.4 4.6 all-to-all-start
  178.0 68.8 %collective-permute-done.1 = bf16[6,384,1024]{2,1,0:T(8,128)(2,1)} collective-permute-done((bf16[6,384,1024]{2,1,0:T(8,128)(2,1)}, bf16[6,384,1024]{2,1,0:T(8,128)(2,1)}, u32[]{:S(2)}, u32[]{:S(2)}) %collective-permute-start.1) | collective-permute-done | bytes 4718624 | tf_op jit(solution)/shard_map/ppermute | solution.py:15
  246.7 20.0 %collective-permute-start.2 = (bf16[6,384,1024]{2,1,0:T(8,128)(2,1)}, bf16[6,384,1024]{2,1,0:T(8,128)(2,1)}, u32[]{:S(2)}, u32[]{:S(2)}) collective-permute-start(bf16[6,384,1024]{2,1,0:T(8,128)(2,1)} %collective-permute-done.1), channel_id=1, source_target_pairs={{0,24},{8,0},{16,8},{24,16},{1,25},{9,1},{17,9},{25,17},{2,26},{10... | collective-permute-start | bytes 14155784 | tf_op jit(solution)/shard_map/ppermute | solution.py:15
  266.7 5.5 constant_dynamic-update-slice_fusion.7
  272.2 5.5 constant_dynamic-update-slice_fusion.6
  277.7 5.6 constant_dynamic-update-slice_fusion.5
  283.4 106.2 %collective-permute-done.2 = bf16[6,384,1024]{2,1,0:T(8,128)(2,1)} collective-permute-done((bf16[6,384,1024]{2,1,0:T(8,128)(2,1)}, bf16[6,384,1024]{2,1,0:T(8,128)(2,1)}, u32[]{:S(2)}, u32[]{:S(2)}) %collective-permute-start.2) | collective-permute-done | bytes 4718624 | tf_op jit(solution)/shard_map/ppermute | solution.py:15
  389.6 5.5 constant_dynamic-update-slice_fusion.4
  395.1 3.2 constant_dynamic-update-slice_fusion.3
  398.4 5.6 constant_dynamic-update-slice_fusion.2
  404.0 5.4 constant_dynamic-update-slice_fusion.1
  409.4 5.5 constant_dynamic-update-slice_fusion
  414.9 12.2 %fusion.12 = f32[8,6,32,1024]{3,2,0,1:T(8,128)} fusion(bf16[8,6,32,1536]{3,2,1,0:T(8,128)(2,1)} %bitcast.11, bf16[6,3072,1024]{2,1,0:T(8,128)(2,1)} %constant_dynamic-update-slice_fusion, s32[]{:T(128)S(6)} %select_n.95), kind=kOutput, calls=%fused_computation.15 | convolution fusion | flops 4831838208 | bytes 29884420 | tf_op jit(solution)/shard_map/jsrd,sdf->jsrf/dot_general | solution.py:104
  427.1 21.3 %all-gather.2.cloned.1.call-done = bf16[6,512,1536]{2,1,0:T(8,128)(2,1)} async-done(((bf16[6,128,1536]{2,1,0:T(8,128)(2,1)}), bf16[6,512,1536]{2,1,0:T(8,128)(2,1)}) %all-gather.2.cloned.1.call-update) | async-done | bytes 9437200 | tf_op jit(solution)/shard_map/all_gather | solution.py:80
  448.4 8.2 %convert_bitcast_fusion = bf16[8,6,32,1536]{3,2,0,1:T(8,128)(2,1)S(1)} fusion(bf16[6,512,1536]{2,1,0:T(8,128)(2,1)} %all-gather.2.cloned.1.call-done, f32[8,6,32,1024]{3,2,0,1:T(8,128)} %fusion.12), kind=kOutput, calls=%fused_computation.10 | convolution fusion | flops 2422996992 | bytes 20447232 | tf_op jit(solution)/shard_map/jsrf,sfd->jsrd/dot_general | solution.py:108
  456.6 2.5 copy.63
  459.1 4.9 all-to-all-start.1
  464.0 0.1 reshape.344
  464.1 0.1 copy.65
  464.2 0.1 reshape.352
  464.4 0.2 fusion.39
  464.6 0.1 select_reduce_fusion.2
  464.7 0.1 copy.58
  464.8 104.3 %all-to-all-done.1 = bf16[48,32,1536]{2,1,0:T(8,128)(2,1)} async-done(((bf16[48,32,1536]{2,1,0:T(8,128)(2,1)}), bf16[48,32,1536]{2,1,0:T(8,128)(2,1)}, u32[]{:S(2)}, u32[]{:S(2)}) %all-to-all-start.1) | async-done | bytes 4718624 | tf_op jit(solution)/shard_map/all_to_all | solution.py:112
  569.1 23.6 %gather_fusion = bf16[1024,1536]{1,0:T(8,128)(2,1)} fusion(bf16[48,32,1536]{2,1,0:T(8,128)(2,1)} %all-to-all-done.1, s32[1024]{0:T(1024)S(1)} %reshape.352), kind=kCustom, calls=%fused_computation | custom fusion | bytes 6299648 | tf_op jit(solution)/shard_map/gather | solution.py:114
  592.8 4.7 fusion.5
  597.5 0.2 fusion.21
  597.7 0.9 fusion.23
  (44 shorter events, 0.4 us)
Async XLA Ops:
  7.2 1.3 copy-start
  7.2 156.3 %reduce-scatter.2.cloned.1.call-start = ((), (), s32[]{:S(2)}) async-start(), calls=%async_computation.3 | async-start | bytes 3932160 | tf_op jit(solution)/shard_map/reduce_scatter | solution.py:84
  8.4 7.7 %copy-start.5 = (s32[128,8]{0,1:T(8,128)S(1)}, s32[128,8]{0,1:T(8,128)}, u32[]{:S(2)}) copy-start(s32[128,8]{0,1:T(8,128)} %param.18) | copy-start | bytes 12292
  8.4 7.9 %copy-start.6 = (s32[48]{0:T(128)S(1)}, s32[48]{0:T(128)}, u32[]{:S(2)}) copy-start(s32[48]{0:T(128)} %param.20) | copy-start | bytes 580
  8.4 8.3 %copy-start.9 = (s32[128,8]{0,1:T(8,128)S(1)}, s32[128,8]{0,1:T(8,128)}, u32[]{:S(2)}) copy-start(s32[128,8]{0,1:T(8,128)} %param.19) | copy-start | bytes 12292
  12.1 140.3 %copy-start.10 = (s32[48]{0:T(128)S(1)}, s32[48]{0:T(128)}, u32[]{:S(2)}) copy-start(s32[48]{0:T(128)} %param.21) | copy-start | bytes 580
  12.1 140.4 %copy-start.12 = (s32[2]{0:T(128)S(1)}, s32[2]{0:T(128)}, u32[]{:S(2)}) copy-start(s32[2]{0:T(128)} %constant.66) | copy-start | bytes 28
  12.1 140.5 %copy-start.11 = (s32[2]{0:T(128)S(1)}, s32[2]{0:T(128)}, u32[]{:S(2)}) copy-start(s32[2]{0:T(128)} %constant.69) | copy-start | bytes 28
  12.1 151.4 %copy-start.3 = (bf16[128,1536]{1,0:T(8,128)(2,1)S(1)}, bf16[128,1536]{1,0:T(8,128)(2,1)}, u32[]{:S(2)}) copy-start(bf16[128,1536]{1,0:T(8,128)(2,1)} %param.14) | copy-start | bytes 1179652
  12.1 152.8 %copy-start.7 = (f32[1536]{0:T(1024)S(1)}, f32[1536]{0:T(1024)}, u32[]{:S(2)}) copy-start(f32[1536]{0:T(1024)} %param.15) | copy-start | bytes 18436
  12.1 436.3 %all-gather.2.cloned.1.call-start = ((), (), s32[]{:S(2)}) async-start(), calls=%async_computation.4 | async-start | bytes 11796480 | tf_op jit(solution)/shard_map/all_gather | solution.py:80
  12.2 122.2 %collective-permute-start = (bf16[6,384,1024]{2,1,0:T(8,128)(2,1)}, bf16[6,384,1024]{2,1,0:T(8,128)(2,1)}, u32[]{:S(2)}, u32[]{:S(2)}) collective-permute-start(bf16[6,384,1024]{2,1,0:T(8,128)(2,1)} %param.22), channel_id=1, source_target_pairs={{0,24},{8,0},{16,8},{24,16},{1,25},{9,1},{17,9},{25,17},{2,26},{10... | collective-permute-start | bytes 14155784 | tf_op jit(solution)/shard_map/ppermute | solution.py:15
  134.4 112.3 %collective-permute-start.1 = (bf16[6,384,1024]{2,1,0:T(8,128)(2,1)}, bf16[6,384,1024]{2,1,0:T(8,128)(2,1)}, u32[]{:S(2)}, u32[]{:S(2)}) collective-permute-start(bf16[6,384,1024]{2,1,0:T(8,128)(2,1)} %collective-permute-done), channel_id=1, source_target_pairs={{0,24},{8,0},{16,8},{24,16},{1,25},{9,1},{17,9},{25,17},{2,26},{10... | collective-permute-start | bytes 14155784 | tf_op jit(solution)/shard_map/ppermute | solution.py:15
  173.4 241.6 %all-to-all-start = ((bf16[48,32,1536]{2,1,0:T(8,128)(2,1)}), bf16[48,32,1536]{2,1,0:T(8,128)(2,1)}, u32[]{:S(2)}, u32[]{:S(2)}) async-start(bf16[48,32,1536]{2,1,0:T(8,128)(2,1)} %bitcast.55), calls=%async_computation.1 | async-start | bytes 9437184 | tf_op jit(solution)/shard_map/all_to_all | solution.py:102
  246.7 142.9 %collective-permute-start.2 = (bf16[6,384,1024]{2,1,0:T(8,128)(2,1)}, bf16[6,384,1024]{2,1,0:T(8,128)(2,1)}, u32[]{:S(2)}, u32[]{:S(2)}) collective-permute-start(bf16[6,384,1024]{2,1,0:T(8,128)(2,1)} %collective-permute-done.1), channel_id=1, source_target_pairs={{0,24},{8,0},{16,8},{24,16},{1,25},{9,1},{17,9},{25,17},{2,26},{10... | collective-permute-start | bytes 14155784 | tf_op jit(solution)/shard_map/ppermute | solution.py:15
  277.7 117.4 %slice-start = ((s8[4718592]{0:T(1024)(128)(4,1)}), s8[4194304]{0:T(1024)(128)(4,1)S(1)}, s32[]{:S(2)}) async-start(s8[4718592]{0:T(1024)(128)(4,1)} %bitcast.53), calls=%async_computation.5 | async-start | bytes 8388608
  283.4 111.7 %slice-start.1 = ((s8[4718592]{0:T(1024)(128)(4,1)}), s8[524288]{0:T(1024)(128)(4,1)S(1)}, s32[]{:S(2)}) async-start(s8[4718592]{0:T(1024)(128)(4,1)} %bitcast.53), calls=%async_computation.6 | async-start | bytes 1048576
  459.1 5.3 copy-start.4
  459.1 110.1 %all-to-all-start.1 = ((bf16[48,32,1536]{2,1,0:T(8,128)(2,1)}), bf16[48,32,1536]{2,1,0:T(8,128)(2,1)}, u32[]{:S(2)}, u32[]{:S(2)}) async-start(bf16[48,32,1536]{2,1,0:T(8,128)(2,1)} %bitcast.56), calls=%async_computation.2 | async-start | bytes 9437184 | tf_op jit(solution)/shard_map/all_to_all | solution.py:112
  569.1 29.5 %copy-start.1 = (bf16[384,1536]{1,0:T(8,128)(2,1)S(1)}, bf16[384,1536]{1,0:T(8,128)(2,1)}, u32[]{:S(2)}) copy-start(bf16[384,1536]{1,0:T(8,128)(2,1)} %param.13) | copy-start | bytes 3538948
  592.8 5.0 copy-start.8
  597.7 0.9 copy-start.2
Sparse Core Ops, SparseCore 0:
  12.3 151.2 reduce-scatter.1
  165.4 282.9 all-gather.1
